TPU v7x, 128 devices: a whole 4x4x4 slice. The times are simulated.
128 devices in a mesh: seq: 16 (over z, y), tp: 8 (over x, core).
Axes of the slice: x: 4, y: 4, z: 4, core: 2. Of those that a mesh axis runs over, the one named last changes fastest.
Arguments:
- hidden: bfloat16 [128, 64, 2560], P(None, 'seq'), may hold values from -6 to 6
- gain_attn: bfloat16 [2560], replicated, may hold values from 0.099609375 to 1.8984375
- w_query: bfloat16 [2560, 2560], P(None, 'tp'), may hold values from -0.125 to 0.125
- w_key: bfloat16 [2560, 640], P(None, 'tp'), may hold values from -0.375 to 0.375
- w_value: bfloat16 [2560, 640], P(None, 'tp'), may hold values from -0.25 to 0.25
- w_out: bfloat16 [2560, 2560], P('tp'), may hold values from -0.125 to 0.125
- gain_ffn: bfloat16 [2560], replicated, may hold values from 0.099609375 to 1.8984375
- w_gate: bfloat16 [2560, 6912], P(None, 'tp'), may hold values from -0.125 to 0.125
- w_up: bfloat16 [2560, 6912], P(None, 'tp'), may hold values from -0.125 to 0.125
- w_down: bfloat16 [6912, 2560], P('tp'), may hold values from -0.078125 to 0.078125
- shared_pages: bfloat16 [320, 8, 2, 80, 128], P('seq', 'tp'), may hold values from -270 to 270
- leaf_pages: bfloat16 [512, 8, 2, 80, 128], P('seq', 'tp'), may hold values from -270 to 270
- root_table: int32 [4, 16], replicated, may hold values from 0 to 319, as said below
- mid_table: int32 [16, 16], replicated, may hold values from 0 to 319, as said below
- leaf_table: int32 [64, 8], replicated, may hold values from 0 to 511, as said below
- root_len: int32 [4], replicated, may hold values from 1024 to 2048, as said below
- mid_len: int32 [16], replicated, may hold values from 1 to 2048, as said below
- leaf_len: int32 [64], replicated, may hold values from 1 to 1024, as said below
- mid_parent: int32 [16], replicated, may hold values from 0 to 3
- leaf_parent: int32 [64], replicated, may hold values from 0 to 15
- slot_request: int32 [64], replicated, may hold values from 0 to 63, as said below
Outputs:
- layer_out: float32 [128, 64, 2560], P('tp', 'seq')
Inputs may be any that keep to these rules, and one draw needn't show every extreme that they name: `slot_request`: A permutation of the requests. The 4 requests of slots 4 * s to 4 * s + 3 have their leaves with 4 distinct owners (see leaf_table). `leaf_table`: all pages of one request's leaf lie with one owner, the index of seq equal to page // 32; each owner holds the leaves of exactly 4 requests, and every leaf page is named once. `root_table`: with mid_table, names every shared page exactly once. Shared page g is held by the index of seq g // 20; each index holds exactly 1 page of every root. `mid_table`: with root_table, names every shared page exactly once. Each index of seq holds exactly 1 page of every middle node. `root_len`: some root reaches the largest value. `mid_len`: some middle node reaches the largest value. `leaf_len`: some leaf reaches the largest value.
All inputs are finite; a program needn't handle non-finite values.
Results may differ from a plain program's by a relative error of at most 0.009.
The roundings to bfloat16 on the way count: a program that leaves them out, or rounds other values in their place, can miss the bound.
Values may be sent and summed in bfloat16 or wider, within the bound.
No kernel may reach another device: no remote copies, remote signals or barrier semaphores. Data moves between devices by JAX's collectives and lax.ppermute only.
A program may use at most 192 MiB of HBM per device.

v0:
```python
import jax
import jax.numpy as jnp
from jax import lax
from jax.sharding import PartitionSpec as P

QH = 32
KVH = 8
HD = 80
WINDOW = 4096
masked_score = -1e30
rope_base = 10000.0


def rms_norm(row_data, gain_vector):
    values = row_data.astype(jnp.float32)
    inverse_rms = lax.rsqrt(jnp.mean(values * values, -1, keepdims=True) + 1e-05)
    return (values * inverse_rms * gain_vector.astype(jnp.float32)).astype(jnp.bfloat16)


def rotate(vector, position):
    half_size = vector.shape[-1] // 2
    frequency = rope_base ** (-2.0 * jnp.arange(half_size, dtype=jnp.float32) / vector.shape[-1])
    angles = position.astype(jnp.float32)[..., None] * frequency
    cos_part = jnp.cos(angles)
    sin_part = jnp.sin(angles)
    first_half = vector[..., :half_size]
    second_half = vector[..., half_size:]
    return jnp.concatenate(
        [
            first_half * cos_part - second_half * sin_part,
            second_half * cos_part + first_half * sin_part,
        ],
        -1,
    )


def page_columns(pages):
    moved = jnp.moveaxis(pages, -5, -2)
    return moved.reshape(moved.shape[:-2] + (moved.shape[-2] * moved.shape[-1],))


def attend(queries, key_pack, key_pos, present, query_pos):
    scores = jnp.einsum(
        "nbkge,bket->nbkgt", queries, key_pack[:, :, 0], preferred_element_type=jnp.float32
    ) * queries.shape[-1] ** (-0.5)
    distance = query_pos[:, :, None] - key_pos[None, :, :]
    allowed = (present[None, :, :] & (distance >= 0) & (distance < WINDOW))[:, :, None, None, :]
    scores = jnp.where(allowed, scores, masked_score)
    maximum = jnp.max(scores, -1)
    weights = jnp.where(allowed, jnp.exp(scores - maximum[..., None]), 0.0)
    totals = jnp.sum(weights, -1)
    weighted = jnp.einsum(
        "nbkgt,bket->nbkge",
        weights.astype(jnp.bfloat16),
        key_pack[:, :, 1],
        preferred_element_type=jnp.float32,
    )
    return (weighted, maximum, totals)


def merge_parts(first, second):
    maximum = jnp.maximum(first[1], second[1])
    first_scale = jnp.exp(first[1] - maximum)
    second_scale = jnp.exp(second[1] - maximum)
    return (
        first[0] * first_scale[..., None] + second[0] * second_scale[..., None],
        maximum,
        first[2] * first_scale + second[2] * second_scale,
    )


def spans(request_ids, root_len, mid_len, leaf_len, mid_parent, leaf_parent):
    mid_nodes = leaf_parent[request_ids]
    root_nodes = mid_parent[mid_nodes]
    return (root_nodes, mid_nodes, root_len[root_nodes], mid_len[mid_nodes], leaf_len[request_ids])


def shards(
    hidden,
    gain_attn,
    w_query,
    w_key,
    w_value,
    w_out,
    gain_ffn,
    w_gate,
    w_up,
    w_down,
    shared_pages,
    leaf_pages,
    root_table,
    mid_table,
    leaf_table,
    root_len,
    mid_len,
    leaf_len,
    mid_parent,
    leaf_parent,
    slot_request,
):
    new_rows, local_reqs, model_width = hidden.shape
    seq_count = lax.axis_size("seq")
    seq_index = lax.axis_index("seq")
    kv_local = leaf_pages.shape[1]
    group_size = QH // KVH
    pages_here = leaf_pages.shape[0]
    slot_ids = seq_index * local_reqs + jnp.arange(local_reqs, dtype=jnp.int32)
    requests = slot_request[slot_ids]
    root_nodes, mid_nodes, root_span, mid_span, leaf_span = spans(
        requests, root_len, mid_len, leaf_len, mid_parent, leaf_parent
    )
    context = root_span + mid_span + leaf_span
    new_index = jnp.arange(new_rows, dtype=jnp.int32)
    query_pos = context[None, :] + new_index[:, None]
    all_slots = slot_request.reshape(seq_count, local_reqs)
    page_store = lax.all_gather(shared_pages, "seq", axis=0, tiled=True)
    root_index = root_table[root_nodes]
    mid_index = mid_table[mid_nodes]
    normed = rms_norm(hidden, gain_attn).reshape(-1, model_width)
    query_proj = jnp.dot(normed, w_query, preferred_element_type=jnp.float32).reshape(
        new_rows, local_reqs, -1, HD
    )
    queries = (
        rotate(query_proj, query_pos[:, :, None])
        .astype(jnp.bfloat16)
        .reshape(new_rows, local_reqs, kv_local, group_size, HD)
    )
    key_proj = jnp.dot(normed, w_key, preferred_element_type=jnp.float32).reshape(
        new_rows, local_reqs, kv_local, HD
    )
    new_keys = rotate(key_proj, query_pos[:, :, None]).astype(jnp.bfloat16)
    new_values = (
        jnp.dot(normed, w_value, preferred_element_type=jnp.float32)
        .astype(jnp.bfloat16)
        .reshape(new_rows, local_reqs, kv_local, HD)
    )
    home_of = leaf_table[:, 0] // pages_here
    own_homes = home_of[requests]
    sender_match = home_of[all_slots] == seq_index
    sender_pick = jnp.argmax(sender_match, 1)
    sender_have = jnp.any(sender_match, 1)
    picked_request = jnp.take_along_axis(all_slots, sender_pick[:, None], 1)[:, 0]
    page_ids = jnp.where(
        sender_have[:, None], leaf_table[picked_request] - seq_index * pages_here, 0
    )
    leaf_steps = jnp.arange(leaf_table.shape[1] * leaf_pages.shape[-1], dtype=jnp.int32)
    fresh_pack = jnp.stack(
        [jnp.transpose(new_keys, (1, 2, 3, 0)), jnp.transpose(new_values, (1, 2, 3, 0))], 2
    )
    fresh_part = attend(
        queries,
        fresh_pack,
        context[:, None] + new_index[None, :],
        jnp.ones((local_reqs, new_rows), bool),
        query_pos,
    )
    outgoing = jnp.where(
        sender_have[:, None, None, None, None, None], jnp.take(leaf_pages, page_ids, axis=0), 0
    )
    arrived = lax.all_to_all(outgoing, "seq", split_axis=0, concat_axis=0, tiled=True)
    leaf_pack = page_columns(jnp.take(arrived, own_homes, axis=0))
    leaf_pos = (root_span + mid_span)[:, None] + leaf_steps[None, :]
    leaf_part = attend(
        queries, leaf_pack, leaf_pos, leaf_steps[None, :] < leaf_span[:, None], query_pos
    )
    root_pack = page_columns(jnp.take(page_store, root_index, axis=0))
    root_steps = jnp.arange(root_pack.shape[-1], dtype=jnp.int32)
    root_part = attend(
        queries,
        root_pack,
        root_steps[None, :] + 0 * root_span[:, None],
        root_steps[None, :] < root_span[:, None],
        query_pos,
    )
    mid_pack = page_columns(jnp.take(page_store, mid_index, axis=0))
    mid_steps = jnp.arange(mid_pack.shape[-1], dtype=jnp.int32)
    mid_part = attend(
        queries,
        mid_pack,
        root_span[:, None] + mid_steps[None, :],
        mid_steps[None, :] < mid_span[:, None],
        query_pos,
    )
    combined = merge_parts(merge_parts(root_part, mid_part), merge_parts(leaf_part, fresh_part))
    attended = (
        (combined[0] / combined[2][..., None])
        .astype(jnp.bfloat16)
        .reshape(new_rows * local_reqs, -1)
    )
    attn_proj = lax.psum(jnp.dot(attended, w_out, preferred_element_type=jnp.float32), "tp")
    resid = hidden.astype(jnp.float32) + attn_proj.reshape(new_rows, local_reqs, model_width)
    normed_ffn = rms_norm(resid, gain_ffn).reshape(-1, model_width)
    gate_rows = jnp.dot(normed_ffn, w_gate, preferred_element_type=jnp.float32)
    up_rows = jnp.dot(normed_ffn, w_up, preferred_element_type=jnp.float32)
    activated = (
        (jax.nn.silu(gate_rows) * up_rows).astype(jnp.bfloat16).reshape(new_rows, local_reqs, -1)
    )
    own_count = new_rows // lax.axis_size("tp")
    ffn_proj = lax.psum_scatter(
        jnp.dot(
            activated.reshape(-1, activated.shape[-1]), w_down, preferred_element_type=jnp.float32
        ).reshape(own_count * lax.axis_size("tp"), local_reqs, model_width),
        "tp",
        scatter_dimension=0,
        tiled=True,
    )
    own_rows = lax.dynamic_slice_in_dim(resid, lax.axis_index("tp") * own_count, own_count, 0)
    return own_rows + ffn_proj


def solution(mesh):
    return jax.shard_map(
        shards,
        mesh=mesh,
        in_specs=(
            P(None, "seq", None),
            P(),
            P(None, "tp"),
            P(None, "tp"),
            P(None, "tp"),
            P("tp", None),
            P(),
            P(None, "tp"),
            P(None, "tp"),
            P("tp", None),
            P("seq", "tp", None, None, None),
            P("seq", "tp", None, None, None),
            P(),
            P(),
            P(),
            P(),
            P(),
            P(),
            P(),
            P(),
            P(),
        ),
        out_specs=P("tp", "seq", None),
        check_vma=False,
    )
```

profile of v0, /device:TPU:1, one launch (start us, length us, event | category | flops | bytes accessed | tf_op | source)
XLA Modules:
  0.0 451.2 jit_solution(16612270365806220123)
XLA Ops:
  6.5 0.7 all-gather.2.cloned.1.call-update
  7.3 0.7 reshape.786
  8.0 0.7 reshape.785
  8.8 0.8 copy.88
  9.6 0.7 and_select_fusion.1
  10.3 0.8 gather_fusion.9
  11.3 0.6 iota_reduce_fusion
  12.0 0.7 gather_fusion.13
  13.6 3.6 gather_fusion.11
  17.2 5.5 %select_select_fusion = bf16[16,8,1,2,80,128]{5,4,3,1,2,0:T(8,128)(2,1)} fusion(bf16[16,8,1,2,80,128]{5,4,3,1,2,0:T(8,128)(2,1)} %bitcast.320, pred[16]{0:T(512)(128)(4,1)S(1)} %reduce_or.9, pred[16,8]{1,0:T(8,128)(4,1)S(1)} %get-tuple-element.17), kind=kLoop, calls=%fused_computation.47 | loop fusion | flops 5242880 | bytes 10485904 | tf_op jit(solution)/shard_map/jit(_where)/select_n | solution.py:157
  22.7 8.8 %all-to-all-start = ((bf16[16,8,1,2,80,128]{5,4,3,1,2,0:T(8,128)(2,1)}), bf16[16,8,1,2,80,128]{5,4,3,1,2,0:T(8,128)(2,1)}, u32[]{:S(2)}, u32[]{:S(2)}) async-start(bf16[16,8,1,2,80,128]{5,4,3,1,2,0:T(8,128)(2,1)} %select_select_fusion), calls=%async_computation | async-start | bytes 10485760 | tf_op jit(solution)/shard_map/all_to_all | solution.py:160
  31.7 0.6 gather_fusion
  32.3 0.6 gather_fusion.8
  33.0 0.6 gather_fusion.6
  33.6 0.6 gather_fusion.1
  34.3 0.6 gather_fusion.5
  34.9 0.6 gather_fusion.2
  36.2 0.6 gather_fusion.4
  37.5 3.4 fusion.17
  40.9 3.0 fusion.19
  44.0 5.8 %reshape.793 = bf16[512,2560]{1,0:T(8,128)(2,1)} reshape(bf16[128,4,2560]{2,1,0:T(4,128)(2,1)} %fusion.19) | data formatting | bytes 5242880 | tf_op jit(solution)/shard_map/reshape | solution.py:119
  49.8 2.6 convolution_convert_fusion
  52.4 0.8 copy.94
  55.5 2.8 fusion.73
  58.4 1.5 fusion.135
  60.4 1.1 fusion.30
  61.6 0.6 copy-done.21
  62.9 0.6 compare_and_fusion.3
  64.8 1.4 fusion.37
  66.5 5.5 %fusion.26 = (pred[128,4,2048]{0,2,1:T(8,128)(4,1)}, pred[128,4,2048]{0,2,1:T(8,128)(4,1)}) fusion(s32[128,4]{0,1:T(4,128)S(1)} %get-tuple-element.29, pred[4,2048]{1,0:T(4,128)(4,1)S(1)} %iota_compare_fusion.1, s32[4,2048]{1,0:T(4,128)S(1)} %iota_add_fusion, pred[4,2048]{1,0:T(4,128)(4,1)S(1)} %iota_compare_fusion), kind=kLoop, calls=%fused_computation.54 | loop fusion | flops 10485760 | bytes 2148352 | tf_op jit(solution)/shard_map/and | solution.py:47
  72.0 55.6 %all-to-all-done = bf16[16,8,1,2,80,128]{5,4,3,1,2,0:T(8,128)(2,1)} async-done(((bf16[16,8,1,2,80,128]{5,4,3,1,2,0:T(8,128)(2,1)}), bf16[16,8,1,2,80,128]{5,4,3,1,2,0:T(8,128)(2,1)}, u32[]{:S(2)}, u32[]{:S(2)}) %all-to-all-start) | async-done | bytes 5242912 | tf_op jit(solution)/shard_map/all_to_all | solution.py:160
  127.6 3.4 gather_fusion.12
  131.0 0.8 fusion.41
  132.3 1.5 reshape.788
  133.8 2.5 fusion.14
  136.3 3.2 copy-done.11
  139.7 2.7 fusion.15
  142.3 16.8 %all-gather.2.cloned.1.call-done = bf16[320,1,2,80,128]{4,3,2,1,0:T(8,128)(2,1)} async-done(((bf16[20,1,2,80,128]{4,3,2,1,0:T(8,128)(2,1)}), bf16[320,1,2,80,128]{4,3,2,1,0:T(8,128)(2,1)}) %all-gather.2.cloned.1.call-update) | async-done | bytes 13107216 | tf_op jit(solution)/shard_map/all_gather | solution.py:116
  159.2 7.1 %gather_fusion.15 = bf16[64,2,80,128]{3,2,1,0:T(8,128)(2,1)} fusion(bf16[320,2,80,128]{3,2,1,0:T(8,128)(2,1)} %bitcast.326, s32[1024]{0:T(1024)S(1)} %copy-done.31), kind=kCustom, calls=%fused_computation.1.clone | custom fusion | bytes 5243136 | tf_op jit(solution)/shard_map/jit(_take)/gather | solution.py:175
  166.2 7.2 %gather_fusion.14 = bf16[64,2,80,128]{3,2,1,0:T(8,128)(2,1)} fusion(bf16[320,2,80,128]{3,2,1,0:T(8,128)(2,1)} %bitcast.327, s32[1024]{0:T(1024)S(1)} %copy-done.30), kind=kCustom, calls=%fused_computation.clone | custom fusion | bytes 5243136 | tf_op jit(solution)/shard_map/jit(_take)/gather | solution.py:166
  173.4 4.2 fusion.35
  177.6 5.2 %reshape.777 = bf16[4,1,2,80,2048]{4,3,0,2,1:T(8,128)(2,1)} reshape(bf16[4,1,2,80,16,128]{5,4,3,0,2,1:T(8,128)(2,1)} %fusion.35) | data formatting | bytes 5242880 | tf_op jit(solution)/shard_map/reshape | solution.py:39
  182.8 4.3 fusion.34
  187.1 5.2 %reshape.781 = bf16[4,1,2,80,2048]{4,3,0,2,1:T(8,128)(2,1)} reshape(bf16[4,1,2,80,16,128]{5,4,3,0,2,1:T(8,128)(2,1)} %fusion.34) | data formatting | bytes 5242880 | tf_op jit(solution)/shard_map/reshape | solution.py:39
  192.3 8.8 %fusion.1 = (f32[128,4,4]{0,2,1:T(4,128)S(1)}, f32[4,2048,128,4]{2,1,3,0:T(8,128)}) fusion(pred[128,4,2048]{0,2,1:T(8,128)(4,1)S(1)} %copy-done.13, bf16[128,4,4,40]{0,3,2,1:T(8,128)(2,1)S(1)} %copy-done.24, bf16[128,4,4,40]{0,3,2,1:T(8,128)(2,1)S(1)} %copy-done.22, bf16[4,1,2,80,2048]{4,3,0,2,1:T(8,128)(2,1)} %reshape.781), kind=kOutput, calls=%fused_computation.21 | convolution fusion | flops 684324864 | bytes 19472384 | tf_op jit(solution)/shard_map/nbkge,bket->nbkgt/dot_general | solution.py:43
  201.1 2.7 fusion
  203.9 10.7 %fusion.2 = (f32[128,4,4]{0,2,1:T(4,128)S(1)}, f32[128,4,4]{0,2,1:T(4,128)S(1)}) fusion(f32[4,2048,128,4]{2,1,3,0:T(8,128)S(1)} %get-tuple-element.38, f32[128,4,4]{0,2,1:T(4,128)S(1)} %get-tuple-element.37, pred[128,4,2048]{0,2,1:T(8,128)(4,1)S(1)} %copy-done.12, f32[128,4,4]{0,2,1:T(4,128)S(1)} %get-tuple-element.31, ...), kind=kLoop, calls=%fused_computation.22 | loop fusion | flops 41938944 | bytes 35684352 | tf_op jit(solution)/shard_map/reduce_sum | solution.py:51
  214.7 3.0 fusion.56
  217.7 10.7 %fusion.68 = f32[128,4,1,4,80]{0,4,3,1,2:T(8,128)} fusion(f32[4,2048,128,4]{2,1,3,0:T(8,128)} %get-tuple-element.32, f32[128,4,4]{0,2,1:T(4,128)S(1)} %get-tuple-element.31, pred[128,4,2048]{0,2,1:T(8,128)(4,1)S(1)} %copy-done.13, bf16[4,1,2,80,2048]{4,3,0,2,1:T(8,128)(2,1)} %reshape.781, f32[128,4,4]{0,2,1:T(4,128)S(1)} %bitcast.342), kind=kOutput, calls=%fused_computation.94 | convolution fusion | flops 692224000 | bytes 19808256 | tf_op jit(solution)/shard_map/nbkgt,bket->nbkge/dot_general | solution.py:52
  228.4 5.8 %fusion.65 = f32[128,4,1,4,80]{0,4,3,1,2:T(8,128)} fusion(f32[128,4,1,4,80]{0,4,3,1,2:T(8,128)} %fusion.68, f32[4,2048,128,4]{2,1,3,0:T(8,128)S(1)} %get-tuple-element.38, f32[128,4,4]{0,2,1:T(4,128)S(1)} %get-tuple-element.37, pred[128,4,2048]{0,2,1:T(8,128)(4,1)S(1)} %copy-done.12, bf16[4,1,2,80,2048]{4,3,0,2,1:T(8,128)(2,1)} %reshape.777, ...), kind=kOutput, calls=%fused_computation.93 | convolution fusion | flops 692551680 | bytes 20471808 | tf_op jit(solution)/shard_map/nbkgt,bket->nbkge/dot_general | solution.py:52
  234.2 1.7 fusion.72
  236.7 3.9 fusion.123
  240.6 7.1 %reshape.798 = f32[128,4,2560]{2,1,0:T(4,128)} reshape(f32[512,2560]{1,0:T(8,128)} %fusion.123) | data formatting | bytes 10485760 | tf_op jit(solution)/shard_map/reshape | solution.py:191
  248.4 76.4 %all-reduce.4.cloned.1.call-done = f32[128,4,2560]{2,1,0:T(4,128)} async-done(((f32[128,4,2560]{2,1,0:T(4,128)}), f32[128,4,2560]{2,1,0:T(4,128)}) %all-reduce.4.cloned.1.call-update) | async-done | bytes 5242896 | tf_op jit(solution)/shard_map/psum | solution.py:190
  324.8 5.1 %multiply_reduce_fusion = (f32[128,4]{1,0:T(8,128)S(1)}, f32[128,4,2560]{2,1,0:T(4,128)S(1)}) fusion(f32[128,4,2560]{2,1,0:T(4,128)} %all-reduce.4.cloned.1.call-done, bf16[128,4,2560]{2,1,0:T(4,128)(2,1)} %param.23), kind=kLoop, calls=%fused_computation.46 | loop fusion | flops 5242368 | bytes 13109248 | tf_op jit(solution)/shard_map/reduce_sum | solution.py:16
  329.9 2.3 copy-done.9
  332.2 2.7 multiply_convert_fusion
  334.9 5.6 %reshape.799 = bf16[512,2560]{1,0:T(8,128)(2,1)} reshape(bf16[128,4,2560]{2,1,0:T(4,128)(2,1)} %multiply_convert_fusion) | data formatting | bytes 5242880 | tf_op jit(solution)/shard_map/reshape | solution.py:192
  340.5 5.5 %fusion.124 = f32[512,864]{0,1:T(8,128)S(1)} fusion(bf16[512,2560]{1,0:T(8,128)(2,1)} %reshape.799, bf16[2560,864]{0,1:T(8,128)(2,1)} %param.30), kind=kOutput, calls=%fused_computation.214 | convolution fusion | flops 2264924160 | bytes 8814592 | tf_op jit(solution)/shard_map/dot_general | solution.py:193
  346.0 12.0 %fusion.78 = f32[512,2560]{1,0:T(8,128)} fusion(bf16[864,2560]{1,0:T(8,128)(2,1)} %param.32, f32[512,864]{0,1:T(8,128)S(1)} %fusion.124, bf16[512,2560]{1,0:T(8,128)(2,1)} %reshape.799, bf16[2560,864]{0,1:T(8,128)(2,1)} %param.31), kind=kOutput, calls=%fused_computation.102 | convolution fusion | flops 4532502528 | bytes 18481152 | tf_op jit(solution)/shard_map/dot_general | solution.py:200
  358.1 7.1 %reshape.800 = f32[128,4,2560]{2,1,0:T(4,128)} reshape(f32[512,2560]{1,0:T(8,128)} %fusion.78) | data formatting | bytes 10485760 | tf_op jit(solution)/shard_map/reshape | solution.py:202
  365.2 0.6 copy-done.38
  367.1 75.0 %all-reduce.6.cloned.1.call-done = f32[128,4,2560]{2,1,0:T(4,128)} async-done(((f32[128,4,2560]{2,1,0:T(4,128)}), f32[128,4,2560]{2,1,0:T(4,128)}) %all-reduce.6.cloned.1.call-update) | async-done | bytes 5242896
  442.1 2.3 dynamic-slice_add_fusion
  (147 shorter events, 10.6 us)
Async XLA Ops:
  6.5 230.2 %copy-start = (bf16[320,2560]{1,0:T(8,128)(2,1)S(1)}, bf16[320,2560]{1,0:T(8,128)(2,1)}, u32[]{:S(2)}) copy-start(bf16[320,2560]{1,0:T(8,128)(2,1)} %param.28) | copy-start | bytes 4915204
  6.5 152.6 %all-gather.2.cloned.1.call-start = ((), (), s32[]{:S(2)}) async-start(), calls=%async_computation.1 | async-start | bytes 13926400 | tf_op jit(solution)/shard_map/all_gather | solution.py:116
  10.3 3.3 copy-start.10
  22.7 9.0 %copy-start.1 = (s32[64]{0:T(128)S(1)}, s32[64]{0:T(128)}, u32[]{:S(2)}) copy-start(s32[64]{0:T(128)} %param.43) | copy-start | bytes 772
  22.7 10.3 %copy-start.2 = (s32[64]{0:T(128)S(1)}, s32[64]{0:T(128)}, u32[]{:S(2)}) copy-start(s32[64]{0:T(128)} %param.40) | copy-start | bytes 772
  22.7 10.9 %copy-start.3 = (s32[64]{0:T(128)S(1)}, s32[64]{0:T(128)}, u32[]{:S(2)}) copy-start(s32[64]{0:T(128)} %param.42) | copy-start | bytes 772
  22.7 11.6 %copy-start.4 = (s32[16]{0:T(128)S(1)}, s32[16]{0:T(128)}, u32[]{:S(2)}) copy-start(s32[16]{0:T(128)} %param.39) | copy-start | bytes 196
  22.7 12.2 %copy-start.5 = (s32[16]{0:T(128)S(1)}, s32[16]{0:T(128)}, u32[]{:S(2)}) copy-start(s32[16]{0:T(128)} %param.41) | copy-start | bytes 196
  22.7 12.9 %copy-start.26 = (s32[16,16]{1,0:T(8,128)S(1)}, s32[16,16]{1,0:T(8,128)}, u32[]{:S(2)}) copy-start(s32[16,16]{1,0:T(8,128)} %param.36) | copy-start | bytes 3076
  22.7 13.5 %copy-start.6 = (s32[4]{0:T(128)S(1)}, s32[4]{0:T(128)}, u32[]{:S(2)}) copy-start(s32[4]{0:T(128)} %param.38) | copy-start | bytes 52
  22.7 14.2 %copy-start.25 = (s32[4,16]{1,0:T(4,128)S(1)}, s32[4,16]{1,0:T(4,128)}, u32[]{:S(2)}) copy-start(s32[4,16]{1,0:T(4,128)} %param.35) | copy-start | bytes 772
  22.7 14.8 %copy-start.32 = (bf16[2560]{0:T(1024)(128)(2,1)S(1)}, bf16[2560]{0:T(1024)(128)(2,1)}, u32[]{:S(2)}) copy-start(bf16[2560]{0:T(1024)(128)(2,1)} %param.24) | copy-start | bytes 15364
  22.7 104.8 %all-to-all-start = ((bf16[16,8,1,2,80,128]{5,4,3,1,2,0:T(8,128)(2,1)}), bf16[16,8,1,2,80,128]{5,4,3,1,2,0:T(8,128)(2,1)}, u32[]{:S(2)}, u32[]{:S(2)}) async-start(bf16[16,8,1,2,80,128]{5,4,3,1,2,0:T(8,128)(2,1)} %select_select_fusion), calls=%async_computation | async-start | bytes 10485760 | tf_op jit(solution)/shard_map/all_to_all | solution.py:160
  31.6 293.2 %all-reduce.4.cloned.1.call-start = ((), (), s32[]{:S(2)}) async-start(), calls=%async_computation.2 | async-start | bytes 10485760 | tf_op jit(solution)/shard_map/psum | solution.py:190
  37.5 3.4 copy-start.7
  40.9 8.9 %copy-start.20 = (bf16[2560,80]{0,1:T(8,128)(2,1)S(1)}, bf16[2560,80]{0,1:T(8,128)(2,1)}, u32[]{:S(2)}) copy-start(bf16[2560,80]{0,1:T(8,128)(2,1)} %param.27) | copy-start | bytes 1228804
  44.0 11.6 %copy-start.37 = (bf16[2560,80]{0,1:T(8,128)(2,1)S(1)}, bf16[2560,80]{0,1:T(8,128)(2,1)}, u32[]{:S(2)}) copy-start(bf16[2560,80]{0,1:T(8,128)(2,1)} %param.26) | copy-start | bytes 1228804
  53.2 5.2 %copy-start.8 = (bf16[128,4,2560]{2,1,0:T(4,128)(2,1)S(1)}, bf16[128,4,2560]{2,1,0:T(4,128)(2,1)}, u32[]{:S(2)}) copy-start(bf16[128,4,2560]{2,1,0:T(4,128)(2,1)} %param.23) | copy-start | bytes 7864324
  55.5 4.9 %copy-start.36 = (bf16[2560,320]{0,1:T(8,128)(2,1)S(1)}, bf16[2560,320]{0,1:T(8,128)(2,1)}, u32[]{:S(2)}) copy-start(bf16[2560,320]{0,1:T(8,128)(2,1)} %param.25) | copy-start | bytes 4915204
  61.6 0.7 copy-start.21
  61.6 1.0 copy-start.23
  62.7 2.1 copy-start.18
  66.2 70.1 %copy-start.15 = (pred[128,4,1024]{0,2,1:T(8,128)(4,1)}, pred[128,4,1024]{0,2,1:T(8,128)(4,1)S(1)}, u32[]{:S(2)}) copy-start(pred[128,4,1024]{0,2,1:T(8,128)(4,1)S(1)} %fusion.37) | copy-start | bytes 1572868
  136.3 3.2 copy-start.11
  136.3 3.3 copy-start.27
  139.7 19.5 %copy-start.31 = (s32[1024]{0:T(1024)S(1)}, s32[1024]{0:T(1024)}, u32[]{:S(2)}) copy-start(s32[1024]{0:T(1024)} %pad_clamp_fusion.4) | copy-start | bytes 12292
  142.3 23.9 %copy-start.30 = (s32[1024]{0:T(1024)S(1)}, s32[1024]{0:T(1024)}, u32[]{:S(2)}) copy-start(s32[1024]{0:T(1024)} %pad_clamp_fusion.5) | copy-start | bytes 12292
  159.2 14.3 %copy-start.35 = (pred[4,16]{1,0:T(4,128)(4,1)S(1)}, pred[4,16]{1,0:T(4,128)(4,1)}, u32[]{:S(2)}) copy-start(pred[4,16]{1,0:T(4,128)(4,1)} %compare_and_fusion.2) | copy-start | bytes 196
  173.4 9.4 %copy-start.34 = (pred[4,16]{1,0:T(4,128)(4,1)S(1)}, pred[4,16]{1,0:T(4,128)(4,1)}, u32[]{:S(2)}) copy-start(pred[4,16]{1,0:T(4,128)(4,1)} %compare_and_fusion.1) | copy-start | bytes 196
  182.8 9.5 %copy-start.13 = (pred[128,4,2048]{0,2,1:T(8,128)(4,1)S(1)}, pred[128,4,2048]{0,2,1:T(8,128)(4,1)}, u32[]{:S(2)}) copy-start(pred[128,4,2048]{0,2,1:T(8,128)(4,1)} %get-tuple-element.28) | copy-start | bytes 3145732
  182.8 9.5 %copy-start.22 = (bf16[128,4,4,40]{0,3,2,1:T(8,128)(2,1)S(1)}, bf16[128,4,4,40]{0,3,2,1:T(8,128)(2,1)}, u32[]{:S(2)}) copy-start(bf16[128,4,4,40]{0,3,2,1:T(8,128)(2,1)} %copy-done.21) | copy-start | bytes 491524
  182.8 9.5 %copy-start.24 = (bf16[128,4,4,40]{0,3,2,1:T(8,128)(2,1)S(1)}, bf16[128,4,4,40]{0,3,2,1:T(8,128)(2,1)}, u32[]{:S(2)}) copy-start(bf16[128,4,4,40]{0,3,2,1:T(8,128)(2,1)} %copy-done.23) | copy-start | bytes 491524
  192.3 8.8 %copy-start.12 = (pred[128,4,2048]{0,2,1:T(8,128)(4,1)S(1)}, pred[128,4,2048]{0,2,1:T(8,128)(4,1)}, u32[]{:S(2)}) copy-start(pred[128,4,2048]{0,2,1:T(8,128)(4,1)} %get-tuple-element.27) | copy-start | bytes 3145732
  192.3 8.8 %copy-start.14 = (bf16[4,1,2,80,2048]{4,3,0,2,1:T(8,128)(2,1)S(1)}, bf16[4,1,2,80,2048]{4,3,0,2,1:T(8,128)(2,1)}, u32[]{:S(2)}) copy-start(bf16[4,1,2,80,2048]{4,3,0,2,1:T(8,128)(2,1)} %reshape.777) | copy-start | bytes 7864324
  201.1 13.6 %slice-start = ((s8[8388608]{0:T(1024)(128)(4,1)}), s8[4194304]{0:T(1024)(128)(4,1)S(1)}, s32[]{:S(2)}) async-start(s8[8388608]{0:T(1024)(128)(4,1)} %bitcast.324), calls=%async_computation.4 | async-start | bytes 8388608
  203.9 10.8 %copy-start.28 = (f32[128,4,4]{0,2,1:T(4,128)S(1)}, f32[128,4,4]{0,2,1:T(4,128)}, u32[]{:S(2)}) copy-start(f32[128,4,4]{0,2,1:T(4,128)} %copy-done.27) | copy-start | bytes 24580
  203.9 10.8 %copy-start.29 = (f32[128,4,4]{0,2,1:T(4,128)S(1)}, f32[128,4,4]{0,2,1:T(4,128)}, u32[]{:S(2)}) copy-start(f32[128,4,4]{0,2,1:T(4,128)} %fusion.15) | copy-start | bytes 24580
  203.9 10.8 %slice-start.1 = ((s8[8388608]{0:T(1024)(128)(4,1)}), s8[4194304]{0:T(1024)(128)(4,1)S(1)}, s32[]{:S(2)}) async-start(s8[8388608]{0:T(1024)(128)(4,1)} %bitcast.324), calls=%async_computation.5 | async-start | bytes 8388608
  203.9 10.8 %copy-start.16 = (pred[128,4,1024]{0,2,1:T(8,128)(4,1)S(1)}, pred[128,4,1024]{0,2,1:T(8,128)(4,1)}, u32[]{:S(2)}) copy-start(pred[128,4,1024]{0,2,1:T(8,128)(4,1)} %copy-done.15) | copy-start | bytes 1572868
  203.9 10.8 %copy-start.17 = (bf16[4,1,2,80,1024]{4,3,0,2,1:T(8,128)(2,1)S(1)}, bf16[4,1,2,80,1024]{4,3,0,2,1:T(8,128)(2,1)}, u32[]{:S(2)}) copy-start(bf16[4,1,2,80,1024]{4,3,0,2,1:T(8,128)(2,1)} %reshape.788) | copy-start | bytes 3932164
  228.4 5.8 %copy-start.19 = (f32[128,4,1,4,128]{0,4,3,1,2:T(8,128)S(1)}, f32[128,4,1,4,128]{0,4,3,1,2:T(8,128)}, u32[]{:S(2)}) copy-start(f32[128,4,1,4,128]{0,4,3,1,2:T(8,128)} %copy-done.18) | copy-start | bytes 3145732
  247.7 0.7 copy-start.33
  247.7 194.3 %all-reduce.6.cloned.1.call-start = ((), (), s32[]{:S(2)}) async-start(), calls=%async_computation.3 | async-start | bytes 10485760
  329.9 2.3 copy-start.9
  365.2 0.7 copy-start.38
Sparse Core Ops, SparseCore 0:
  9.5 149.6 all-gather.1
  247.8 76.8 all-reduce.3
  365.3 76.6 all-reduce.5
where the time goes:
time: 457 us; the launch traced here: 451 us
  waiting for transfers between devices  225 us (49%)
  local copies, waits for them, and re-layouts  79.4 us (17%)
  matrix products  63.6 us (14%)
  other arithmetic  60 us (13%)
  between operations  14.6 us (3%)
  starting transfers between devices  8.91 us (2%)
    psum x1, waiting for transfers between devices, shards(): lax.psum(jnp.dot(attended, w_out, preferred_element_type=jnp.float32), 'tp')  76.4 us
    unnamed x4, waiting for transfers between devices  75.7 us
    all_to_all x1, waiting for transfers between devices, shards(): lax.all_to_all(outgoing, 'seq', split_axis=0, concat_axis=0, tiled=True)  55.6 us
    dot_general x4, matrix products, attend(): jnp.einsum('nbkgt,bket->nbkge', weights.astype(jnp.bfloat16), key_pack[:,...  21.1 us
    all_gather x1, waiting for transfers between devices, shards(): page_store = lax.all_gather(shared_pages, 'seq', axis=0, tiled=True)  16.8 us
    dot_general x4, matrix products, attend(): jnp.einsum('nbkge,bket->nbkgt', queries, key_pack[:, :, 0], preferred_ele...  14.5 us
    reduce_sum x3, other arithmetic, attend(): totals = jnp.sum(weights, -1)  13.6 us
    dot_general x1, matrix products, shards(): jnp.dot(activated.reshape(-1, activated.shape[-1]), w_down, preferred_ele...  12 us
  transfers between devices with their start and end apart: 4, of which 4 were waited for; matrix products, arithmetic and copies ran while one was open for 15% of the time, Pallas kernels for 0%

commit v1 on v0

--- a/solution.py
+++ b/solution.py
@@ -187,7 +187,9 @@
         .astype(jnp.bfloat16)
         .reshape(new_rows * local_reqs, -1)
     )
-    attn_proj = lax.psum(jnp.dot(attended, w_out, preferred_element_type=jnp.float32), "tp")
+    attn_proj = jnp.sum(
+        lax.all_gather(jnp.dot(attended, w_out, preferred_element_type=jnp.float32), "tp"), axis=0
+    )
     resid = hidden.astype(jnp.float32) + attn_proj.reshape(new_rows, local_reqs, model_width)
     normed_ffn = rms_norm(resid, gain_ffn).reshape(-1, model_width)
     gate_rows = jnp.dot(normed_ffn, w_gate, preferred_element_type=jnp.float32)

time: 457 us -> 591 us (1.29)
  waiting for transfers between devices: 225 us -> 340 us
  other arithmetic: 60 us -> 78.9 us
    all_gather x0 -> x1, waiting for transfers between devices: none -> 193 us  [shards(): lax.all_gather(jnp.dot(attended, w_out, preferred_element_type=jnp.float3...]
    psum x1 -> x0, waiting for transfers between devices: 76.4 us -> none  [shards(): lax.psum(jnp.dot(attended, w_out, preferred_element_type=jnp.float32), 'tp')]
    reduce_sum x0 -> x1, other arithmetic: none -> 18.9 us  [shards(): jnp.sum(lax.all_gather(jnp.dot(attended, w_out, preferred_element_type=jn...]
  transfers between devices with their start and end apart: 4 -> 4, of which waited for: 4 -> 4; matrix products, arithmetic and copies ran while one was open for 15% -> 11% of each run, Pallas kernels for 0% -> 0%
where the time goes in v1:
time: 591 us; the launch traced here: 585 us
  waiting for transfers between devices  340 us (58%)
  local copies, waits for them, and re-layouts  79.1 us (13%)
  other arithmetic  78.9 us (13%)
  matrix products  63.6 us (11%)
  between operations  14.6 us (2%)
  starting transfers between devices  8.91 us (2%)
    all_gather x1, waiting for transfers between devices, shards(): lax.all_gather(jnp.dot(attended, w_out, preferred_element_type=jnp.float3...  193 us
    unnamed x4, waiting for transfers between devices  74.1 us
    all_to_all x1, waiting for transfers between devices, shards(): lax.all_to_all(outgoing, 'seq', split_axis=0, concat_axis=0, tiled=True)  55.7 us
    dot_general x4, matrix products, attend(): jnp.einsum('nbkgt,bket->nbkge', weights.astype(jnp.bfloat16), key_pack[:,...  21.1 us
    reduce_sum x1, other arithmetic, shards(): jnp.sum(lax.all_gather(jnp.dot(attended, w_out, preferred_element_type=jn...  18.9 us
    all_gather x1, waiting for transfers between devices, shards(): page_store = lax.all_gather(shared_pages, 'seq', axis=0, tiled=True)  16.8 us
    dot_general x4, matrix products, attend(): jnp.einsum('nbkge,bket->nbkgt', queries, key_pack[:, :, 0], preferred_ele...  14.5 us
    reduce_sum x3, other arithmetic, attend(): totals = jnp.sum(weights, -1)  13.6 us
  transfers between devices with their start and end apart: 4, of which 4 were waited for; matrix products, arithmetic and copies ran while one was open for 11% of the time, Pallas kernels for 0%

profile of v1, /device:TPU:1, one launch (start us, length us, event | category | flops | bytes accessed | tf_op | source)
XLA Modules:
  0.0 585.1 jit_solution(18383533720909590489)
XLA Ops:
  6.5 0.7 all-gather.4.cloned.1.call-update
  7.3 0.7 reshape.786
  8.0 0.7 reshape.785
  8.8 0.8 copy.88
  9.6 0.7 and_select_fusion.1
  10.3 0.8 gather_fusion.9
  11.3 0.6 iota_reduce_fusion
  12.0 0.7 gather_fusion.13
  13.6 3.6 gather_fusion.11
  17.2 5.5 select_select_fusion
  22.7 8.8 %all-to-all-start = ((bf16[16,8,1,2,80,128]{5,4,3,1,2,0:T(8,128)(2,1)}), bf16[16,8,1,2,80,128]{5,4,3,1,2,0:T(8,128)(2,1)}, u32[]{:S(2)}, u32[]{:S(2)}) async-start(bf16[16,8,1,2,80,128]{5,4,3,1,2,0:T(8,128)(2,1)} %select_select_fusion), calls=%async_computation | async-start | bytes 10485760 | tf_op jit(solution)/shard_map/all_to_all | solution.py:160
  31.7 0.6 gather_fusion
  32.3 0.6 gather_fusion.8
  33.0 0.6 gather_fusion.6
  33.6 0.6 gather_fusion.1
  34.3 0.6 gather_fusion.5
  34.9 0.6 gather_fusion.2
  36.2 0.6 gather_fusion.4
  37.5 3.4 fusion.17
  40.9 3.0 fusion.19
  44.0 5.8 reshape.793
  49.7 2.6 convolution_convert_fusion
  52.4 0.8 copy.94
  55.5 2.8 fusion.73
  58.3 1.5 fusion.135
  60.3 1.1 fusion.30
  61.6 0.6 copy-done.21
  62.8 0.6 compare_and_fusion.3
  64.7 1.4 fusion.37
  66.4 5.5 fusion.26
  71.9 55.7 %all-to-all-done = bf16[16,8,1,2,80,128]{5,4,3,1,2,0:T(8,128)(2,1)} async-done(((bf16[16,8,1,2,80,128]{5,4,3,1,2,0:T(8,128)(2,1)}), bf16[16,8,1,2,80,128]{5,4,3,1,2,0:T(8,128)(2,1)}, u32[]{:S(2)}, u32[]{:S(2)}) %all-to-all-start) | async-done | bytes 5242912 | tf_op jit(solution)/shard_map/all_to_all | solution.py:160
  127.6 3.4 gather_fusion.12
  131.0 0.8 fusion.41
  132.3 1.5 reshape.788
  133.8 2.5 fusion.14
  136.3 3.2 copy-done.11
  139.7 2.7 fusion.15
  142.3 16.8 %all-gather.4.cloned.1.call-done = bf16[320,1,2,80,128]{4,3,2,1,0:T(8,128)(2,1)} async-done(((bf16[20,1,2,80,128]{4,3,2,1,0:T(8,128)(2,1)}), bf16[320,1,2,80,128]{4,3,2,1,0:T(8,128)(2,1)}) %all-gather.4.cloned.1.call-update) | async-done | bytes 13107216 | tf_op jit(solution)/shard_map/all_gather | solution.py:116
  159.2 7.1 %gather_fusion.15 = bf16[64,2,80,128]{3,2,1,0:T(8,128)(2,1)} fusion(bf16[320,2,80,128]{3,2,1,0:T(8,128)(2,1)} %bitcast.328, s32[1024]{0:T(1024)S(1)} %copy-done.31), kind=kCustom, calls=%fused_computation.1.clone | custom fusion | bytes 5243136 | tf_op jit(solution)/shard_map/jit(_take)/gather | solution.py:175
  166.2 7.2 %gather_fusion.14 = bf16[64,2,80,128]{3,2,1,0:T(8,128)(2,1)} fusion(bf16[320,2,80,128]{3,2,1,0:T(8,128)(2,1)} %bitcast.329, s32[1024]{0:T(1024)S(1)} %copy-done.30), kind=kCustom, calls=%fused_computation.clone | custom fusion | bytes 5243136 | tf_op jit(solution)/shard_map/jit(_take)/gather | solution.py:166
  173.4 4.2 fusion.35
  177.6 5.2 reshape.777
  182.8 4.3 fusion.34
  187.1 5.2 reshape.781
  192.3 8.8 %fusion.1 = (f32[128,4,4]{0,2,1:T(4,128)S(1)}, f32[4,2048,128,4]{2,1,3,0:T(8,128)}) fusion(pred[128,4,2048]{0,2,1:T(8,128)(4,1)S(1)} %copy-done.13, bf16[128,4,4,40]{0,3,2,1:T(8,128)(2,1)S(1)} %copy-done.24, bf16[128,4,4,40]{0,3,2,1:T(8,128)(2,1)S(1)} %copy-done.22, bf16[4,1,2,80,2048]{4,3,0,2,1:T(8,128)(2,1)} %reshape.781), kind=kOutput, calls=%fused_computation.21 | convolution fusion | flops 684324864 | bytes 19472384 | tf_op jit(solution)/shard_map/nbkge,bket->nbkgt/dot_general | solution.py:43
  201.1 2.7 fusion
  203.9 10.7 %fusion.2 = (f32[128,4,4]{0,2,1:T(4,128)S(1)}, f32[128,4,4]{0,2,1:T(4,128)S(1)}) fusion(f32[4,2048,128,4]{2,1,3,0:T(8,128)S(1)} %get-tuple-element.38, f32[128,4,4]{0,2,1:T(4,128)S(1)} %get-tuple-element.37, pred[128,4,2048]{0,2,1:T(8,128)(4,1)S(1)} %copy-done.12, f32[128,4,4]{0,2,1:T(4,128)S(1)} %get-tuple-element.31, ...), kind=kLoop, calls=%fused_computation.22 | loop fusion | flops 41938944 | bytes 35684352 | tf_op jit(solution)/shard_map/reduce_sum | solution.py:51
  214.7 3.0 fusion.56
  217.7 10.7 %fusion.68 = f32[128,4,1,4,80]{0,4,3,1,2:T(8,128)} fusion(f32[4,2048,128,4]{2,1,3,0:T(8,128)} %get-tuple-element.32, f32[128,4,4]{0,2,1:T(4,128)S(1)} %get-tuple-element.31, pred[128,4,2048]{0,2,1:T(8,128)(4,1)S(1)} %copy-done.13, bf16[4,1,2,80,2048]{4,3,0,2,1:T(8,128)(2,1)} %reshape.781, f32[128,4,4]{0,2,1:T(4,128)S(1)} %bitcast.344), kind=kOutput, calls=%fused_computation.94 | convolution fusion | flops 692224000 | bytes 19808256 | tf_op jit(solution)/shard_map/nbkgt,bket->nbkge/dot_general | solution.py:52
  228.4 5.8 fusion.65
  234.2 1.7 fusion.72
  236.7 3.9 fusion.123
  241.3 193.2 %all-gather.6.cloned.1.call-done = f32[4096,2560]{1,0:T(8,128)} async-done(((f32[512,2560]{1,0:T(8,128)}), f32[4096,2560]{1,0:T(8,128)}) %all-gather.6.cloned.1.call-update) | async-done | bytes 41943056 | tf_op jit(solution)/shard_map/all_gather | solution.py:191
  434.5 18.9 %reduce_sum.68 = f32[512,2560]{1,0:T(8,128)} reduce(f32[8,512,2560]{2,1,0:T(8,128)} %bitcast.321, f32[]{:T(128)} %constant.58.clone.1), dimensions={0}, to_apply=%region_11.13 | reduce | flops 9175040 | bytes 47185924 | tf_op jit(solution)/shard_map/reduce_sum | solution.py:190
  453.4 7.1 %reshape.798 = f32[128,4,2560]{2,1,0:T(4,128)} reshape(f32[512,2560]{1,0:T(8,128)} %reduce_sum.68) | data formatting | bytes 10485760 | tf_op jit(solution)/shard_map/reshape | solution.py:193
  460.5 5.1 multiply_reduce_fusion
  465.7 2.3 copy-done.9
  467.9 2.7 multiply_convert_fusion
  470.7 5.3 reshape.799
  476.0 5.5 fusion.124
  481.6 12.0 %fusion.78 = f32[512,2560]{1,0:T(8,128)} fusion(bf16[864,2560]{1,0:T(8,128)(2,1)} %param.32, f32[512,864]{0,1:T(8,128)S(1)} %fusion.124, bf16[512,2560]{1,0:T(8,128)(2,1)} %reshape.799, bf16[2560,864]{0,1:T(8,128)(2,1)} %param.31), kind=kOutput, calls=%fused_computation.102 | convolution fusion | flops 4532502528 | bytes 18481152 | tf_op jit(solution)/shard_map/dot_general | solution.py:202
  493.6 7.1 %reshape.800 = f32[128,4,2560]{2,1,0:T(4,128)} reshape(f32[512,2560]{1,0:T(8,128)} %fusion.78) | data formatting | bytes 10485760 | tf_op jit(solution)/shard_map/reshape | solution.py:204
  502.6 73.4 %all-reduce.3.cloned.1.call-done = f32[128,4,2560]{2,1,0:T(4,128)} async-done(((f32[128,4,2560]{2,1,0:T(4,128)}), f32[128,4,2560]{2,1,0:T(4,128)}) %all-reduce.3.cloned.1.call-update) | async-done | bytes 5242896
  576.0 2.3 dynamic-slice_add_fusion
  (148 shorter events, 11.2 us)
Async XLA Ops:
  6.5 230.2 %copy-start = (bf16[320,2560]{1,0:T(8,128)(2,1)S(1)}, bf16[320,2560]{1,0:T(8,128)(2,1)}, u32[]{:S(2)}) copy-start(bf16[320,2560]{1,0:T(8,128)(2,1)} %param.28) | copy-start | bytes 4915204
  6.5 152.6 %all-gather.4.cloned.1.call-start = ((), (), s32[]{:S(2)}) async-start(), calls=%async_computation.1 | async-start | bytes 13926400 | tf_op jit(solution)/shard_map/all_gather | solution.py:116
  10.3 3.3 copy-start.10
  22.7 9.0 %copy-start.1 = (s32[64]{0:T(128)S(1)}, s32[64]{0:T(128)}, u32[]{:S(2)}) copy-start(s32[64]{0:T(128)} %param.43) | copy-start | bytes 772
  22.7 10.3 %copy-start.2 = (s32[64]{0:T(128)S(1)}, s32[64]{0:T(128)}, u32[]{:S(2)}) copy-start(s32[64]{0:T(128)} %param.40) | copy-start | bytes 772
  22.7 10.9 %copy-start.3 = (s32[64]{0:T(128)S(1)}, s32[64]{0:T(128)}, u32[]{:S(2)}) copy-start(s32[64]{0:T(128)} %param.42) | copy-start | bytes 772
  22.7 11.6 %copy-start.4 = (s32[16]{0:T(128)S(1)}, s32[16]{0:T(128)}, u32[]{:S(2)}) copy-start(s32[16]{0:T(128)} %param.39) | copy-start | bytes 196
  22.7 12.2 %copy-start.5 = (s32[16]{0:T(128)S(1)}, s32[16]{0:T(128)}, u32[]{:S(2)}) copy-start(s32[16]{0:T(128)} %param.41) | copy-start | bytes 196
  22.7 12.9 %copy-start.26 = (s32[16,16]{1,0:T(8,128)S(1)}, s32[16,16]{1,0:T(8,128)}, u32[]{:S(2)}) copy-start(s32[16,16]{1,0:T(8,128)} %param.36) | copy-start | bytes 3076
  22.7 13.5 %copy-start.6 = (s32[4]{0:T(128)S(1)}, s32[4]{0:T(128)}, u32[]{:S(2)}) copy-start(s32[4]{0:T(128)} %param.38) | copy-start | bytes 52
  22.7 14.2 %copy-start.25 = (s32[4,16]{1,0:T(4,128)S(1)}, s32[4,16]{1,0:T(4,128)}, u32[]{:S(2)}) copy-start(s32[4,16]{1,0:T(4,128)} %param.35) | copy-start | bytes 772
  22.7 14.8 %copy-start.32 = (bf16[2560]{0:T(1024)(128)(2,1)S(1)}, bf16[2560]{0:T(1024)(128)(2,1)}, u32[]{:S(2)}) copy-start(bf16[2560]{0:T(1024)(128)(2,1)} %param.24) | copy-start | bytes 15364
  22.7 104.8 %all-to-all-start = ((bf16[16,8,1,2,80,128]{5,4,3,1,2,0:T(8,128)(2,1)}), bf16[16,8,1,2,80,128]{5,4,3,1,2,0:T(8,128)(2,1)}, u32[]{:S(2)}, u32[]{:S(2)}) async-start(bf16[16,8,1,2,80,128]{5,4,3,1,2,0:T(8,128)(2,1)} %select_select_fusion), calls=%async_computation | async-start | bytes 10485760 | tf_op jit(solution)/shard_map/all_to_all | solution.py:160
  31.6 402.9 %all-gather.6.cloned.1.call-start = ((), (), s32[]{:S(2)}) async-start(), calls=%async_computation.2 | async-start | bytes 47185920 | tf_op jit(solution)/shard_map/all_gather | solution.py:191
  37.5 3.4 copy-start.7
  40.9 8.8 %copy-start.20 = (bf16[2560,80]{0,1:T(8,128)(2,1)S(1)}, bf16[2560,80]{0,1:T(8,128)(2,1)}, u32[]{:S(2)}) copy-start(bf16[2560,80]{0,1:T(8,128)(2,1)} %param.27) | copy-start | bytes 1228804
  44.0 11.5 %copy-start.37 = (bf16[2560,80]{0,1:T(8,128)(2,1)S(1)}, bf16[2560,80]{0,1:T(8,128)(2,1)}, u32[]{:S(2)}) copy-start(bf16[2560,80]{0,1:T(8,128)(2,1)} %param.26) | copy-start | bytes 1228804
  53.1 5.2 copy-start.8
  55.5 4.9 copy-start.36
  61.5 0.7 copy-start.21
  61.6 1.0 copy-start.23
  62.6 2.1 copy-start.18
  66.2 70.2 %copy-start.15 = (pred[128,4,1024]{0,2,1:T(8,128)(4,1)}, pred[128,4,1024]{0,2,1:T(8,128)(4,1)S(1)}, u32[]{:S(2)}) copy-start(pred[128,4,1024]{0,2,1:T(8,128)(4,1)S(1)} %fusion.37) | copy-start | bytes 1572868
  136.3 3.2 copy-start.11
  136.3 3.3 copy-start.27
  139.7 19.5 %copy-start.31 = (s32[1024]{0:T(1024)S(1)}, s32[1024]{0:T(1024)}, u32[]{:S(2)}) copy-start(s32[1024]{0:T(1024)} %pad_clamp_fusion.4) | copy-start | bytes 12292
  142.3 23.9 %copy-start.30 = (s32[1024]{0:T(1024)S(1)}, s32[1024]{0:T(1024)}, u32[]{:S(2)}) copy-start(s32[1024]{0:T(1024)} %pad_clamp_fusion.5) | copy-start | bytes 12292
  159.2 14.3 %copy-start.35 = (pred[4,16]{1,0:T(4,128)(4,1)S(1)}, pred[4,16]{1,0:T(4,128)(4,1)}, u32[]{:S(2)}) copy-start(pred[4,16]{1,0:T(4,128)(4,1)} %compare_and_fusion.2) | copy-start | bytes 196
  173.4 9.4 %copy-start.34 = (pred[4,16]{1,0:T(4,128)(4,1)S(1)}, pred[4,16]{1,0:T(4,128)(4,1)}, u32[]{:S(2)}) copy-start(pred[4,16]{1,0:T(4,128)(4,1)} %compare_and_fusion.1) | copy-start | bytes 196
  182.8 9.5 %copy-start.13 = (pred[128,4,2048]{0,2,1:T(8,128)(4,1)S(1)}, pred[128,4,2048]{0,2,1:T(8,128)(4,1)}, u32[]{:S(2)}) copy-start(pred[128,4,2048]{0,2,1:T(8,128)(4,1)} %get-tuple-element.28) | copy-start | bytes 3145732
  182.8 9.5 %copy-start.22 = (bf16[128,4,4,40]{0,3,2,1:T(8,128)(2,1)S(1)}, bf16[128,4,4,40]{0,3,2,1:T(8,128)(2,1)}, u32[]{:S(2)}) copy-start(bf16[128,4,4,40]{0,3,2,1:T(8,128)(2,1)} %copy-done.21) | copy-start | bytes 491524
  182.8 9.5 %copy-start.24 = (bf16[128,4,4,40]{0,3,2,1:T(8,128)(2,1)S(1)}, bf16[128,4,4,40]{0,3,2,1:T(8,128)(2,1)}, u32[]{:S(2)}) copy-start(bf16[128,4,4,40]{0,3,2,1:T(8,128)(2,1)} %copy-done.23) | copy-start | bytes 491524
  192.3 8.8 %copy-start.12 = (pred[128,4,2048]{0,2,1:T(8,128)(4,1)S(1)}, pred[128,4,2048]{0,2,1:T(8,128)(4,1)}, u32[]{:S(2)}) copy-start(pred[128,4,2048]{0,2,1:T(8,128)(4,1)} %get-tuple-element.27) | copy-start | bytes 3145732
  192.3 8.8 %copy-start.14 = (bf16[4,1,2,80,2048]{4,3,0,2,1:T(8,128)(2,1)S(1)}, bf16[4,1,2,80,2048]{4,3,0,2,1:T(8,128)(2,1)}, u32[]{:S(2)}) copy-start(bf16[4,1,2,80,2048]{4,3,0,2,1:T(8,128)(2,1)} %reshape.777) | copy-start | bytes 7864324
  201.1 13.6 %slice-start = ((s8[8388608]{0:T(1024)(128)(4,1)}), s8[4194304]{0:T(1024)(128)(4,1)S(1)}, s32[]{:S(2)}) async-start(s8[8388608]{0:T(1024)(128)(4,1)} %bitcast.326), calls=%async_computation.4 | async-start | bytes 8388608
  203.9 10.8 %copy-start.28 = (f32[128,4,4]{0,2,1:T(4,128)S(1)}, f32[128,4,4]{0,2,1:T(4,128)}, u32[]{:S(2)}) copy-start(f32[128,4,4]{0,2,1:T(4,128)} %copy-done.27) | copy-start | bytes 24580
  203.9 10.8 %copy-start.29 = (f32[128,4,4]{0,2,1:T(4,128)S(1)}, f32[128,4,4]{0,2,1:T(4,128)}, u32[]{:S(2)}) copy-start(f32[128,4,4]{0,2,1:T(4,128)} %fusion.15) | copy-start | bytes 24580
  203.9 10.8 %slice-start.1 = ((s8[8388608]{0:T(1024)(128)(4,1)}), s8[4194304]{0:T(1024)(128)(4,1)S(1)}, s32[]{:S(2)}) async-start(s8[8388608]{0:T(1024)(128)(4,1)} %bitcast.326), calls=%async_computation.5 | async-start | bytes 8388608
  203.9 10.8 %copy-start.16 = (pred[128,4,1024]{0,2,1:T(8,128)(4,1)S(1)}, pred[128,4,1024]{0,2,1:T(8,128)(4,1)}, u32[]{:S(2)}) copy-start(pred[128,4,1024]{0,2,1:T(8,128)(4,1)} %copy-done.15) | copy-start | bytes 1572868
  203.9 10.8 %copy-start.17 = (bf16[4,1,2,80,1024]{4,3,0,2,1:T(8,128)(2,1)S(1)}, bf16[4,1,2,80,1024]{4,3,0,2,1:T(8,128)(2,1)}, u32[]{:S(2)}) copy-start(bf16[4,1,2,80,1024]{4,3,0,2,1:T(8,128)(2,1)} %reshape.788) | copy-start | bytes 3932164
  228.4 5.8 copy-start.19
  240.6 0.7 copy-start.33
  240.6 335.4 %all-reduce.3.cloned.1.call-start = ((), (), s32[]{:S(2)}) async-start(), calls=%async_computation.3 | async-start | bytes 10485760
  465.6 2.3 copy-start.9
  500.7 0.7 copy-start.38
Sparse Core Ops, SparseCore 0:
  9.5 149.6 all-gather.3
  240.8 193.7 all-gather.5
  500.9 75.0 all-reduce.2
